TPU v7x, 32 devices: a whole 2x2x4 slice. The times are simulated.
32 devices in a mesh: dp: 8 (over z, y), tensor: 4 (over x, core).
Axes of the slice: x: 2, y: 2, z: 4, core: 2. Of those that a mesh axis runs over, the one named last changes fastest.
Arguments:
- hidden_in: bfloat16 [32768, 768], P(('dp', 'tensor')), may hold values from -6 to 6
- qkv_weight: bfloat16 [3, 768, 768], P(None, 'tensor'), may hold values from -0.21875 to 0.21875
- qv_bias: bfloat16 [2, 768], P(None, 'tensor'), may hold values from -3 to 3
- out_weight: bfloat16 [768, 768], P('tensor'), may hold values from -1.25 to 1.25
- out_bias: bfloat16 [768], replicated, may hold values from -3 to 3
- norm1_gain: bfloat16 [768], replicated, may hold values from 0.25 to 1.75
- norm1_shift: bfloat16 [768], replicated, may hold values from -3 to 3
- up_weight: bfloat16 [3072, 768], P('tensor'), may hold values from -0.21875 to 0.21875
- up_bias: bfloat16 [3072], P('tensor'), may hold values from -3 to 3
- down_weight: bfloat16 [3072, 768], P('tensor'), may hold values from -0.109375 to 0.109375
- down_bias: bfloat16 [768], replicated, may hold values from -3 to 3
- norm2_gain: bfloat16 [768], replicated, may hold values from 0.25 to 1.75
- norm2_shift: bfloat16 [768], replicated, may hold values from -3 to 3
- out_grad: bfloat16 [32768, 768], P(('dp', 'tensor')), may hold values from -12 to 12
- seq_lengths: int32 [256], P('dp'), may hold values from 32 to 128, as said below
- key_mask: int32 [32768], P('dp'), may hold values 0 or 1
- split_pos: int32 [256], P('dp'), may hold values from 8 to 95, as said below
Outputs:
- layer_out: bfloat16 [32768, 768], P(('dp', 'tensor'))
- input_grad: bfloat16 [32768, 768], P(('dp', 'tensor'))
- grad_qkv_weight: float32 [3, 768, 768], P(None, 'tensor')
- grad_qv_bias: float32 [2, 768], P(None, 'tensor')
- grad_out_weight: float32 [768, 768], P('tensor')
- grad_out_bias: float32 [768], replicated
- grad_norm1_gain: float32 [768], replicated
- grad_norm1_shift: float32 [768], replicated
- grad_up_weight: float32 [3072, 768], P('tensor')
- grad_up_bias: float32 [3072], P('tensor')
- grad_down_weight: float32 [3072, 768], P('tensor')
- grad_down_bias: float32 [768], replicated
- grad_norm2_gain: float32 [768], replicated
- grad_norm2_shift: float32 [768], replicated
Inputs may be any that keep to these rules, and one draw needn't show every extreme that they name: `seq_lengths`: every slot's length is at least a quarter of 128; the first slot of each index of dp is full. `split_pos`: a slot's split position is at least its length // 4 (a quarter, rounded down) and below three quarters of it.
All inputs are finite; a program needn't handle non-finite values. No bound on the sum of `key_mask` on one device may be relied on, other than what follows from the above.
Results may differ from a plain program's by a relative error of at most 0.019.
Values may be sent and summed in bfloat16 or wider, within the bound.
No kernel may reach another device: no remote copies, remote signals or barrier semaphores. Data moves between devices by JAX's collectives and lax.ppermute only.
A program may use at most 192 MiB of HBM per device.

v0:
```python
import jax
import jax.numpy as jnp
from jax import lax
from jax.sharding import PartitionSpec as P

HD = 64
EPSILON = 1e-05
ROOT_HALF = 0.7071067811865476
DENSITY = 0.3989422804014327
F32 = jnp.float32
BF16 = jnp.bfloat16


def norm_forward(hidden, norm_gain, norm_offset):
    average = jnp.mean(hidden, axis=1, keepdims=True)
    centred = hidden - average
    spread = jnp.mean(centred * centred, axis=1, keepdims=True)
    inverse = lax.rsqrt(spread + EPSILON)
    normal = centred * inverse
    return (normal * norm_gain + norm_offset, normal, inverse)


def norm_backward(upstream, normal, inverse, norm_gain):
    scaled = upstream * norm_gain
    first_mean = jnp.mean(scaled, axis=1, keepdims=True)
    second_mean = jnp.mean(scaled * normal, axis=1, keepdims=True)
    return inverse * (scaled - first_mean - normal * second_mean)


def gelu_parts(before):
    cumulative = 0.5 * (1.0 + jax.scipy.special.erf(before * ROOT_HALF))
    density = DENSITY * jnp.exp(-0.5 * before * before)
    return (before * cumulative, cumulative + before * density)


def body(
    hidden_in,
    qkv_weight,
    qv_bias,
    out_weight,
    out_bias,
    norm1_gain,
    norm1_shift,
    up_weight,
    up_bias,
    down_weight,
    down_bias,
    norm2_gain,
    norm2_shift,
    out_grad,
    seq_lengths,
    key_mask,
    split_pos,
):
    rows = hidden_in.shape[0]
    part_count = lax.axis_size("tensor")
    part_index = lax.axis_index("tensor")
    group_slots = seq_lengths.shape[0]
    slot_len = rows * part_count // group_slots
    slots = rows // slot_len
    width = hidden_in.shape[1]
    heads = width // HD
    w_qkv = lax.all_gather(qkv_weight, "tensor", axis=1, tiled=True)
    b_qv = lax.all_gather(qv_bias, "tensor", axis=1, tiled=True)
    w_out = lax.all_gather(out_weight, "tensor", axis=0, tiled=True)
    w_up = lax.all_gather(up_weight, "tensor", axis=0, tiled=True)
    b_up = lax.all_gather(up_bias, "tensor", axis=0, tiled=True)
    w_down = lax.all_gather(down_weight, "tensor", axis=0, tiled=True)
    lengths = lax.dynamic_slice_in_dim(seq_lengths, part_index * slots, slots)
    splits = lax.dynamic_slice_in_dim(split_pos, part_index * slots, slots)
    mask = lax.dynamic_slice_in_dim(key_mask, part_index * rows, rows).reshape(slots, slot_len)
    places = lax.broadcasted_iota(jnp.int32, (slots, slot_len), 1)
    valid = (places < lengths[:, None]) & ((mask == 1) | (places == 0))
    target = (
        ((places >= splits[:, None]) & (places < lengths[:, None])).astype(F32).reshape(rows, 1)
    )
    gain_mid = norm1_gain.astype(F32)
    shift_mid = norm1_shift.astype(F32)
    gain_out = norm2_gain.astype(F32)
    shift_out = norm2_shift.astype(F32)
    projected = jnp.einsum("rd,cld->crl", hidden_in, w_qkv, preferred_element_type=F32)
    bias_rows = jnp.stack([b_qv[0], jnp.zeros_like(b_qv[0]), b_qv[1]]).astype(F32)
    projected = (projected + bias_rows[:, None, :]).astype(BF16)
    head_shape = (slots, slot_len, heads, HD)
    queries = projected[0].reshape(head_shape)
    key_rows = projected[1].reshape(head_shape)
    value_rows = projected[2].reshape(head_shape)
    scores = jnp.einsum("sqhe,skhe->shqk", queries, key_rows, preferred_element_type=F32) * HD ** (
        -0.5
    )
    masked = jnp.where(valid[:, None, None, :], scores, -1e30)
    largest = jnp.max(masked, axis=-1, keepdims=True)
    weights_raw = jnp.exp(masked - largest)
    totals = jnp.sum(weights_raw, axis=-1, keepdims=True)
    probability = weights_raw / totals
    prob_low = probability.astype(BF16)
    context = jnp.einsum("shqk,skhe->sqhe", prob_low, value_rows, preferred_element_type=F32)
    context_rows = context.astype(BF16).reshape(rows, width)
    attn_out = jnp.dot(context_rows, w_out, preferred_element_type=F32)
    first_sum = hidden_in.astype(F32) + attn_out + out_bias.astype(F32)
    mid_rows, mid_normal, mid_inverse = norm_forward(first_sum, gain_mid, shift_mid)
    mid_low = mid_rows.astype(BF16)
    before = jnp.einsum("rd,fd->rf", mid_low, w_up, preferred_element_type=F32) + b_up.astype(F32)
    activated, gelu_slope = gelu_parts(before)
    activated_low = activated.astype(BF16)
    ffn_out = jnp.dot(activated_low, w_down, preferred_element_type=F32)
    second_sum = mid_rows + ffn_out + down_bias.astype(F32)
    out_rows, out_normal, out_inverse = norm_forward(second_sum, gain_out, shift_out)
    layer_out = out_rows.astype(BF16)
    upstream = out_grad.astype(F32) * target
    grad_gain_out = jnp.sum(upstream * out_normal, axis=0)
    grad_shift_out = jnp.sum(upstream, axis=0)
    second_grad = norm_backward(upstream, out_normal, out_inverse, gain_out)
    grad_down_bias = jnp.sum(second_grad, axis=0)
    second_low = second_grad.astype(BF16)
    grad_down = jnp.einsum("rf,rd->fd", activated_low, second_low, preferred_element_type=F32)
    grad_down = lax.psum(
        lax.psum_scatter(grad_down, "tensor", scatter_dimension=0, tiled=True), "dp"
    )
    activated_grad = jnp.einsum("rd,fd->rf", second_low, w_down, preferred_element_type=F32)
    before_low = (activated_grad * gelu_slope).astype(BF16)
    grad_up = jnp.einsum("rf,rd->fd", before_low, mid_low, preferred_element_type=F32)
    grad_up_bias = jnp.sum(before_low, axis=0, dtype=F32)
    grad_up = lax.psum(lax.psum_scatter(grad_up, "tensor", scatter_dimension=0, tiled=True), "dp")
    grad_up_bias = lax.psum(
        lax.psum_scatter(grad_up_bias, "tensor", scatter_dimension=0, tiled=True), "dp"
    )
    mid_grad = second_grad + jnp.dot(before_low, w_up, preferred_element_type=F32)
    grad_gain_mid = jnp.sum(mid_grad * mid_normal, axis=0)
    grad_shift_mid = jnp.sum(mid_grad, axis=0)
    first_grad = norm_backward(mid_grad, mid_normal, mid_inverse, gain_mid)
    grad_out_bias = jnp.sum(first_grad, axis=0)
    first_low = first_grad.astype(BF16)
    grad_out_weight = jnp.einsum("rl,rd->ld", context_rows, first_low, preferred_element_type=F32)
    grad_out_weight = lax.psum(
        lax.psum_scatter(grad_out_weight, "tensor", scatter_dimension=0, tiled=True), "dp"
    )
    context_grad = (
        jnp.einsum("rd,ld->rl", first_low, w_out, preferred_element_type=F32)
        .astype(BF16)
        .reshape(head_shape)
    )
    prob_grad = jnp.einsum("sqhe,skhe->shqk", context_grad, value_rows, preferred_element_type=F32)
    inner_sum = jnp.sum(probability * prob_grad, axis=-1, keepdims=True)
    score_grad = (probability * (prob_grad - inner_sum)).astype(BF16)
    query_grad = jnp.einsum(
        "shqk,skhe->sqhe", score_grad, key_rows, preferred_element_type=F32
    ) * HD ** (-0.5)
    key_grad = jnp.einsum(
        "shqk,sqhe->skhe", score_grad, queries, preferred_element_type=F32
    ) * HD ** (-0.5)
    value_grad = jnp.einsum("shqk,sqhe->skhe", prob_low, context_grad, preferred_element_type=F32)
    projected_grad = jnp.stack(
        [
            query_grad.reshape(rows, width),
            key_grad.reshape(rows, width),
            value_grad.reshape(rows, width),
        ]
    ).astype(BF16)
    grad_qkv = jnp.einsum("crl,rd->cld", projected_grad, hidden_in, preferred_element_type=F32)
    bias_sums = jnp.sum(projected_grad, axis=1, dtype=F32)
    grad_qv_bias = jnp.stack([bias_sums[0], bias_sums[2]])
    input_grad = (
        first_grad + jnp.einsum("crl,cld->rd", projected_grad, w_qkv, preferred_element_type=F32)
    ).astype(BF16)
    grad_qkv = lax.psum(lax.psum_scatter(grad_qkv, "tensor", scatter_dimension=1, tiled=True), "dp")
    grad_qv_bias = lax.psum(
        lax.psum_scatter(grad_qv_bias, "tensor", scatter_dimension=1, tiled=True), "dp"
    )
    grad_out_bias, grad_gain_mid, grad_shift_mid, grad_down_bias, grad_gain_out, grad_shift_out = (
        lax.psum(
            (
                grad_out_bias,
                grad_gain_mid,
                grad_shift_mid,
                grad_down_bias,
                grad_gain_out,
                grad_shift_out,
            ),
            ("dp", "tensor"),
        )
    )
    return (
        layer_out,
        input_grad,
        grad_qkv,
        grad_qv_bias,
        grad_out_weight,
        grad_out_bias,
        grad_gain_mid,
        grad_shift_mid,
        grad_up,
        grad_up_bias,
        grad_down,
        grad_down_bias,
        grad_gain_out,
        grad_shift_out,
    )


def solution(mesh):
    in_specs = (
        P(("dp", "tensor"), None),
        P(None, "tensor", None),
        P(None, "tensor"),
        P("tensor", None),
        P(),
        P(),
        P(),
        P("tensor", None),
        P("tensor"),
        P("tensor", None),
        P(),
        P(),
        P(),
        P(("dp", "tensor"), None),
        P("dp"),
        P("dp"),
        P("dp"),
    )
    out_specs = (
        P(("dp", "tensor"), None),
        P(("dp", "tensor"), None),
        P(None, "tensor", None),
        P(None, "tensor"),
        P("tensor", None),
        P(),
        P(),
        P(),
        P("tensor", None),
        P("tensor"),
        P("tensor", None),
        P(),
        P(),
        P(),
    )
    return jax.shard_map(body, mesh=mesh, in_specs=in_specs, out_specs=out_specs, check_vma=False)
```

profile of v0, /device:TPU:0, one launch (start us, length us, event | category | flops | bytes accessed | tf_op | source)
XLA Modules:
  0.0 752.3 jit_solution(9560384906454295733)
XLA Ops:
  10.3 6.0 all-gather
  17.2 1.6 copy.80
  18.9 5.5 all-gather.1
  26.2 16.9 %all-gather.7.cloned.1.call-done = bf16[3,768,768]{2,1,0:T(8,128)(2,1)} async-done(((bf16[3,192,768]{2,1,0:T(8,128)(2,1)}), bf16[3,768,768]{2,1,0:T(8,128)(2,1)}) %all-gather.7.cloned.1.call-update) | async-done | bytes 3538960 | tf_op jit(solution)/shard_map/all_gather | solution.py:63
  43.2 6.1 fusion.8
  53.0 2.7 fusion.64
  58.3 2.4 copy.86
  62.2 3.8 fusion.65
  66.4 34.8 %all-gather.11.cloned.1.call-done = bf16[3072,768]{1,0:T(8,128)(2,1)} async-done(((bf16[768,768]{1,0:T(8,128)(2,1)}), bf16[3072,768]{1,0:T(8,128)(2,1)}) %all-gather.11.cloned.1.call-update) | async-done | bytes 4718608 | tf_op jit(solution)/shard_map/all_gather | solution.py:66
  101.2 12.8 %multiply_convert_fusion = (bf16[1024,3072]{1,0:T(8,128)(2,1)}, f32[1024,3072]{1,0:T(8,128)}) fusion(f32[3072]{0:T(1024)S(1)} %bitcast.117, bf16[3072,768]{1,0:T(8,128)(2,1)} %all-gather.11.cloned.1.call-done, f32[1024,768]{0,1:T(8,128)S(1)} %get-tuple-element.92, f32[768]{0:T(1024)S(1)} %convert_element_type.102, f32[768]{0:T(1024)S(1)} %convert_element_type.101, ...), kind=kOutput, calls=%fused_computation.9 | convolution fusion | flops 4854644736 | bytes 26765312 | tf_op jit(solution)/shard_map/rd,fd->rf/dot_general | solution.py:103
  114.1 26.0 %all-gather.13.cloned.1.call-done = bf16[3072,768]{1,0:T(8,128)(2,1)} async-done(((bf16[768,768]{1,0:T(8,128)(2,1)}), bf16[3072,768]{1,0:T(8,128)(2,1)}) %all-gather.13.cloned.1.call-update) | async-done | bytes 4718608 | tf_op jit(solution)/shard_map/all_gather | solution.py:68
  140.1 9.4 %fusion.66 = (f32[1024]{0:T(1024)S(1)}, f32[1024,768]{0,1:T(8,128)S(1)}) fusion(f32[768]{0:T(1024)S(1)} %convert_element_type.106, bf16[1024,3072]{1,0:T(8,128)(2,1)} %get-tuple-element.93, bf16[3072,768]{1,0:T(8,128)(2,1)} %all-gather.13.cloned.1.call-done, f32[768]{0:T(1024)S(1)} %convert_element_type.102, f32[768]{0:T(1024)S(1)} %convert_element_type.101, ...), kind=kOutput, calls=%fused_computation.113 | convolution fusion | flops 4837342208 | bytes 17323008 | tf_op jit(solution)/shard_map/dot_general | solution.py:106
  152.4 12.6 %convert_reduce_fusion = (f32[3072]{0:T(1024)S(1)}, bf16[1024,3072]{1,0:T(8,128)(2,1)}) fusion(f32[1024,3072]{1,0:T(8,128)} %get-tuple-element.94, f32[3072]{0:T(1024)S(1)} %bitcast.118, bf16[3072,768]{1,0:T(8,128)(2,1)S(1)} %copy-done.26, f32[1024]{0:T(1024)S(1)} %get-tuple-element.102, f32[1024,768]{0,1:T(8,128)S(1)} %get-tuple-element.96, ...), kind=kOutput, calls=%fused_computation.8 | convolution fusion | flops 4880593920 | bytes 28359680 | tf_op jit(solution)/shard_map/rd,fd->rf/dot_general | solution.py:120
  165.0 11.2 %multiply_reduce_fusion.2 = (f32[768]{0:T(1024)S(1)}, f32[1024]{0:T(1024)S(1)}, f32[1024]{0:T(1024)S(1)}, f32[768]{0:T(1024)S(1)}, f32[1024,768]{0,1:T(8,128)S(1)}) fusion(f32[1024,768]{0,1:T(8,128)S(1)} %copy-done.6, f32[1024]{0:T(1024)S(1)} %add_rsqrt_fusion.1, f32[1024]{0:T(1024)S(1)} %broadcast_multiply_fusion.5, f32[768]{0:T(1024)S(1)} %convert_element_type.101, ...), kind=kOutput, calls=%fused_computation.23 | convolution fusion | flops 4846776320 | bytes 22069248 | tf_op jit(solution)/shard_map/dot_general | solution.py:128
  177.4 1.6 copy-done.8
  179.0 2.8 fusion.17
  181.9 4.8 convolution_convert_fusion.1
  186.8 2.8 copy.90
  189.5 2.1 copy.124
  191.7 7.5 multiply_reduce_fusion
  199.2 5.0 multiply_convert_fusion.1
  205.9 2.4 copy.95
  208.3 3.7 stack_reshape.12
  212.0 2.6 copy.102
  214.6 4.6 fusion.26
  219.2 2.4 copy.98
  221.6 3.7 stack_reshape.13
  225.3 2.8 copy.103
  228.1 5.5 fusion.30
  233.6 2.4 copy.101
  236.1 3.7 stack_reshape.14
  239.7 2.6 copy.104
  242.3 9.7 %fusion.20 = f32[3,768,768]{2,1,0:T(8,128)} fusion(bf16[1024,768]{1,0:T(8,128)(2,1)} %param.17, bf16[1,1024,768]{2,1,0:T(8,128)(2,1)} %copy.104, bf16[1,1024,768]{2,1,0:T(8,128)(2,1)} %copy.103, bf16[1,1024,768]{2,1,0:T(8,128)(2,1)} %copy.102), kind=kOutput, calls=%fused_computation.58 | convolution fusion | flops 3628597248 | bytes 13369344 | tf_op jit(solution)/shard_map/crl,rd->cld/dot_general | solution.py:160
  252.1 11.7 %fusion.47 = f32[3072,768]{1,0:T(8,128)} fusion(bf16[1024,3072]{1,0:T(8,128)(2,1)} %get-tuple-element.93, bf16[1024,768]{0,1:T(8,128)(2,1)} %copy.88, f32[1024,768]{0,1:T(8,128)S(1)} %get-tuple-element.96, f32[1024]{0:T(1024)S(1)} %get-tuple-element.102, f32[1024]{0:T(1024)S(1)} %get-tuple-element.103, f32[1024]{0:T(1024)S(1)} %get-tuple-element.87, ...), kind=kOutput, calls=%fused_computation.81 | convolution fusion | flops 4839702528 | bytes 20470784 | tf_op jit(solution)/shard_map/rf,rd->fd/dot_general | solution.py:116
  263.9 11.9 %fusion.56 = f32[3072,768]{1,0:T(8,128)} fusion(bf16[1024,3072]{1,0:T(8,128)(2,1)} %get-tuple-element.101, f32[1024,768]{0,1:T(8,128)} %copy-done.5, f32[768]{0:T(1024)S(1)} %convert_element_type.102, f32[768]{0:T(1024)S(1)} %convert_element_type.101, f32[1024]{0:T(1024)S(1)} %add_rsqrt_fusion.1, f32[1024]{0:T(1024)S(1)} %broadcast_multiply_fusion.5), kind=kOutput, calls=%fused_computation.105 | convolution fusion | flops 4835770368 | bytes 18888704 | tf_op jit(solution)/shard_map/rf,rd->fd/dot_general | solution.py:122
  275.9 2.7 convert_reduce_fusion.1
  279.6 36.0 %reduce-scatter.8.cloned.1.call-done = f32[3,192,768]{2,1,0:T(8,128)} async-done(((f32[3,768,768]{2,1,0:T(8,128)}), f32[3,192,768]{2,1,0:T(8,128)}) %reduce-scatter.8.cloned.1.call-update) | async-done | bytes 1769488 | tf_op jit(solution)/shard_map/reduce_scatter | solution.py:166
  315.7 80.5 %reduce-scatter.14.cloned.1.call-done = f32[768,768]{1,0:T(8,128)} async-done(((f32[3072,768]{1,0:T(8,128)}), f32[768,768]{1,0:T(8,128)}) %reduce-scatter.14.cloned.1.call-update) | async-done | bytes 2359312 | tf_op jit(solution)/shard_map/reduce_scatter | solution.py:118
  396.2 80.6 %reduce-scatter.12.cloned.1.call-done = f32[768,768]{1,0:T(8,128)} async-done(((f32[3072,768]{1,0:T(8,128)}), f32[768,768]{1,0:T(8,128)}) %reduce-scatter.12.cloned.1.call-update) | async-done | bytes 2359312 | tf_op jit(solution)/shard_map/reduce_scatter | solution.py:124
  478.7 9.3 %fusion.9 = bf16[1024,768]{0,1:T(8,128)(2,1)} fusion(f32[1024,768]{0,1:T(8,128)} %copy-done.8, bf16[3,768,768]{2,1,0:T(8,128)(2,1)} %all-gather.7.cloned.1.call-done, bf16[1,1024,768]{2,1,0:T(8,128)(2,1)} %copy.104, bf16[1,1024,768]{2,1,0:T(8,128)(2,1)} %copy.103, bf16[1,1024,768]{2,1,0:T(8,128)(2,1)} %copy.102), kind=kOutput, calls=%fused_computation.21 | convolution fusion | flops 3630170112 | bytes 12976128 | tf_op jit(solution)/shard_map/crl,cld->rd/dot_general | solution.py:164
  488.0 2.6 copy.108
  490.6 4.2 multiply_reduce_fusion.1
  494.9 2.6 copy.107
  497.5 10.1 %all-reduce = f32[3072]{0:T(1024)S(1)} all-reduce(f32[3072]{0:T(1024)S(1)} %get-tuple-element.100), channel_id=6, replica_groups=mesh['dp'=8,'tensor'=4] {'tensor'}, use_global_device_ids=true, to_apply=%region_27.28.clone | all-reduce | flops 3072 | bytes 24576
  507.6 45.4 %all-reduce.1 = (f32[768]{0:T(1024)}, f32[768]{0:T(1024)}, f32[768]{0:T(1024)}, f32[768]{0:T(1024)}, f32[768]{0:T(1024)}, /*index=5*/f32[768]{0:T(1024)}) all-reduce(f32[768]{0:T(1024)S(1)} %get-tuple-element.77, f32[768]{0:T(1024)S(1)} %get-tuple-element.56, ...), channel_id=1, replica_groups=mesh['dp'=8,'tensor'=4] {'dp','tensor'}, use_global_device_ids=true, to_apply=%region_19.20 | all-reduce | flops 4608 | bytes 36864 | tf_op jit(solution)/shard_map/psum | solution.py:171
  554.0 23.0 %all-reduce.2 = (f32[2,192]{1,0:T(2,128)}, f32[768]{0:T(1024)}) all-reduce(f32[2,192]{1,0:T(2,128)S(1)} %copy.119, f32[768]{0:T(1024)S(1)} %dynamic-slice.1), channel_id=1, replica_groups=mesh['dp'=8,'tensor'=4] {'dp'}, use_global_device_ids=true, to_apply=%region_15.16 | all-reduce | flops 1152 | bytes 9216 | tf_op jit(solution)/shard_map/psum | solution.py:167
  577.0 161.4 %all-reduce.6.cloned.1.call-done = (f32[3,192,768]{2,1,0:T(8,128)}, f32[192,768]{1,0:T(8,128)}, f32[768,768]{1,0:T(8,128)}, f32[768,768]{1,0:T(8,128)}) async-done(((f32[3,192,768]{2,1,0:T(8,128)}, f32[192,768]{1,0:T(8,128)}, f32[768,768]{1,0:T(8,128)}, f32[768,768]{1,0:T(8,128)}), (f32[3,192,768]{2,1,0:T(8,128)}, f32[192,768]{1,0:T(8,128)}, f32[768,768]{1,0:T(8,128)}, ...) | async-done | bytes 7077904 | tf_op jit(solution)/shard_map/psum | solution.py:166
  738.4 2.9 copy.159
  (132 shorter events, 26.7 us)
Async XLA Ops:
  7.2 3.0 copy-start.27
  7.2 3.0 copy-start.28
  7.2 3.1 copy-start.25
  7.2 10.0 %copy-start.12 = (bf16[1024,768]{1,0:T(8,128)(2,1)S(1)}, bf16[1024,768]{1,0:T(8,128)(2,1)}, u32[]{:S(2)}) copy-start(bf16[1024,768]{1,0:T(8,128)(2,1)} %param.17) | copy-start | bytes 4718596
  7.2 35.9 %all-gather.7.cloned.1.call-start = ((), (), s32[]{:S(2)}) async-start(), calls=%async_computation.5 | async-start | bytes 4423680 | tf_op jit(solution)/shard_map/all_gather | solution.py:63
  8.0 10.9 %copy-start.18 = (bf16[768]{0:T(1024)(128)(2,1)S(1)}, bf16[768]{0:T(1024)(128)(2,1)}, u32[]{:S(2)}) copy-start(bf16[768]{0:T(1024)(128)(2,1)} %param.21) | copy-start | bytes 4612
  8.0 10.9 %copy-start.19 = (bf16[768]{0:T(1024)(128)(2,1)S(1)}, bf16[768]{0:T(1024)(128)(2,1)}, u32[]{:S(2)}) copy-start(bf16[768]{0:T(1024)(128)(2,1)} %param.22) | copy-start | bytes 4612
  8.0 10.9 %copy-start.20 = (bf16[768]{0:T(1024)(128)(2,1)S(1)}, bf16[768]{0:T(1024)(128)(2,1)}, u32[]{:S(2)}) copy-start(bf16[768]{0:T(1024)(128)(2,1)} %param.23) | copy-start | bytes 4612
  8.0 10.9 %copy-start.24 = (bf16[768]{0:T(1024)(128)(2,1)S(1)}, bf16[768]{0:T(1024)(128)(2,1)}, u32[]{:S(2)}) copy-start(bf16[768]{0:T(1024)(128)(2,1)} %param.25) | copy-start | bytes 4612
  8.0 16.4 %copy-start.21 = (bf16[768]{0:T(1024)(128)(2,1)S(1)}, bf16[768]{0:T(1024)(128)(2,1)}, u32[]{:S(2)}) copy-start(bf16[768]{0:T(1024)(128)(2,1)} %param.27) | copy-start | bytes 4612
  8.0 16.4 %copy-start.11 = (bf16[1024,768]{1,0:T(8,128)(2,1)S(1)}, bf16[1024,768]{1,0:T(8,128)(2,1)}, u32[]{:S(2)}) copy-start(bf16[1024,768]{1,0:T(8,128)(2,1)} %param.30) | copy-start | bytes 4718596
  8.0 54.2 %all-gather.9.cloned.1.call-start = ((), (), s32[]{:S(2)}) async-start(), calls=%async_computation.6 | async-start | bytes 1474560 | tf_op jit(solution)/shard_map/all_gather | solution.py:65
  8.8 92.4 %all-gather.11.cloned.1.call-start = ((), (), s32[]{:S(2)}) async-start(), calls=%async_computation.7 | async-start | bytes 5898240 | tf_op jit(solution)/shard_map/all_gather | solution.py:66
  9.5 130.6 %all-gather.13.cloned.1.call-start = ((), (), s32[]{:S(2)}) async-start(), calls=%async_computation.8 | async-start | bytes 5898240 | tf_op jit(solution)/shard_map/all_gather | solution.py:68
  10.1 269.6 %reduce-scatter.10.cloned.1.call-start = ((), (), s32[]{:S(2)}) async-start(), calls=%async_computation.10 | async-start | bytes 2949120 | tf_op jit(solution)/shard_map/reduce_scatter | solution.py:136
  17.2 8.9 %copy-start.22 = (bf16[768]{0:T(1024)(128)(2,1)S(1)}, bf16[768]{0:T(1024)(128)(2,1)}, u32[]{:S(2)}) copy-start(bf16[768]{0:T(1024)(128)(2,1)} %param.28) | copy-start | bytes 4612
  50.8 1.2 copy-start.1
  51.3 1.8 copy-start.2
  51.7 4.0 copy-start.13
  55.7 2.6 copy-start.7
  66.0 48.0 %copy-start.5 = (f32[1024,768]{0,1:T(8,128)}, f32[1024,768]{0,1:T(8,128)S(1)}, u32[]{:S(2)}) copy-start(f32[1024,768]{0,1:T(8,128)S(1)} %get-tuple-element.92) | copy-start | bytes 9437188
  149.5 1.4 copy-start.4
  149.9 2.5 copy-start.26
  152.4 12.6 %copy-start.6 = (f32[1024,768]{0,1:T(8,128)S(1)}, f32[1024,768]{0,1:T(8,128)}, u32[]{:S(2)}) copy-start(f32[1024,768]{0,1:T(8,128)} %copy-done.5) | copy-start | bytes 9437188
  176.2 2.8 copy-start.15
  177.4 1.6 copy-start.8
  181.9 133.8 %reduce-scatter.8.cloned.1.call-start = ((), (), s32[]{:S(2)}) async-start(), calls=%async_computation.9 | async-start | bytes 8847360 | tf_op jit(solution)/shard_map/reduce_scatter | solution.py:166
  189.5 2.1 copy-start.14
  191.6 7.6 %copy-start.16 = (bf16[96,8,8,128]{3,2,1,0:T(8,128)(2,1)}, bf16[96,8,8,128]{3,2,1,0:T(8,128)(2,1)S(1)}, u32[]{:S(2)}) copy-start(bf16[96,8,8,128]{3,2,1,0:T(8,128)(2,1)S(1)} %copy.124) | copy-start | bytes 4718596
  191.7 7.6 %slice-start = ((s8[6291456]{0:T(1024)(128)(4,1)}), s8[4194304]{0:T(1024)(128)(4,1)S(1)}, s32[]{:S(2)}) async-start(s8[6291456]{0:T(1024)(128)(4,1)} %bitcast.106), calls=%async_computation.15 | async-start | bytes 8388608
  191.7 7.5 %slice-start.1 = ((s8[6291456]{0:T(1024)(128)(4,1)}), s8[2097152]{0:T(1024)(128)(4,1)S(1)}, s32[]{:S(2)}) async-start(s8[6291456]{0:T(1024)(128)(4,1)} %bitcast.106), calls=%async_computation.16 | async-start | bytes 4194304
  199.2 5.0 copy-start.3
  204.2 1.7 copy-start
  252.0 144.2 %reduce-scatter.14.cloned.1.call-start = ((), (), s32[]{:S(2)}) async-start(), calls=%async_computation.12 | async-start | bytes 11796480 | tf_op jit(solution)/shard_map/reduce_scatter | solution.py:118
  263.8 212.9 %reduce-scatter.12.cloned.1.call-start = ((), (), s32[]{:S(2)}) async-start(), calls=%async_computation.11 | async-start | bytes 11796480 | tf_op jit(solution)/shard_map/reduce_scatter | solution.py:124
  275.8 277.2 %reduce-scatter.16.cloned.1.call-start = ((), (), s32[]{:S(2)}) async-start(), calls=%async_computation.13 | async-start | bytes 491520
  279.6 458.8 %all-reduce.6.cloned.1.call-start = ((), (), s32[]{:S(2)}) async-start(), calls=%async_computation.14 | async-start | bytes 14155776 | tf_op jit(solution)/shard_map/psum | solution.py:166
  476.8 0.7 copy-start.23
  476.8 0.7 copy-start.29
  738.4 3.0 copy-start.17
  738.4 3.8 copy-start.10
  741.4 2.2 copy-start.9
Sparse Core Ops, SparseCore 0:
  9.6 33.5 all-gather.6
  44.7 17.4 all-gather.8
  63.7 37.4 all-gather.10
  102.6 37.4 all-gather.12
  182.0 32.7 reduce-scatter.9
  252.2 63.4 reduce-scatter.7
  318.3 77.8 reduce-scatter.13
  398.8 77.9 reduce-scatter.11
  479.8 20.8 reduce-scatter.15
  505.0 233.3 all-reduce.5
where the time goes:
time: 761 us; the launch traced here: 752 us
  waiting for transfers between devices  440 us (58%)
  matrix products  127 us (17%)
  blocking collectives  90 us (12%)
  local copies, waits for them, and re-layouts  60.4 us (8%)
  other arithmetic  18.2 us (2%)
  between operations  15.8 us (2%)
    psum x1, waiting for transfers between devices, body(): lax.psum(lax.psum_scatter(grad_qkv, 'tensor', scatter_dimension=1, tiled=...  161 us
    reduce_scatter x1, waiting for transfers between devices, body(): lax.psum_scatter(grad_up, 'tensor', scatter_dimension=0, tiled=True)  80.6 us
    reduce_scatter x1, waiting for transfers between devices, body(): lax.psum_scatter(grad_down, 'tensor', scatter_dimension=0, tiled=True)  80.5 us
    psum x1, blocking collectives, body(): lax.psum((grad_out_bias, grad_gain_mid, grad_shift_mid, grad_down_bias, g...  45.4 us
    reduce_scatter x1, waiting for transfers between devices, body(): lax.psum_scatter(grad_qkv, 'tensor', scatter_dimension=1, tiled=True)  36 us
    all_gather x1, waiting for transfers between devices, body(): w_up = lax.all_gather(up_weight, 'tensor', axis=0, tiled=True)  34.8 us
    unnamed x83, local copies, waits for them, and re-layouts  28.7 us
    all_gather x1, waiting for transfers between devices, body(): w_down = lax.all_gather(down_weight, 'tensor', axis=0, tiled=True)  26 us
  transfers between devices with their start and end apart: 10, of which 8 were waited for; matrix products, arithmetic and copies ran while one was open for 20% of the time, Pallas kernels for 0%

commit v1 on v0

--- a/solution.py
+++ b/solution.py
@@ -163,7 +163,8 @@
     input_grad = (
         first_grad + jnp.einsum("crl,cld->rd", projected_grad, w_qkv, preferred_element_type=F32)
     ).astype(BF16)
-    grad_qkv = lax.psum(lax.psum_scatter(grad_qkv, "tensor", scatter_dimension=1, tiled=True), "dp")
+    array_here = lax.psum_scatter(grad_qkv, "tensor", scatter_dimension=1, tiled=True)
+    grad_qkv = lax.all_gather(array_here, axis_name="dp").sum(axis=0)
     grad_qv_bias = lax.psum(
         lax.psum_scatter(grad_qv_bias, "tensor", scatter_dimension=1, tiled=True), "dp"
     )

time: 761 us -> 938 us (1.23)
  waiting for transfers between devices: 440 us -> 614 us
    all_gather x0 -> x1, waiting for transfers between devices: none -> 124 us  [body(): grad_qkv = lax.all_gather(array_here, axis_name='dp').sum(axis=0)]
    reduce_scatter x1, waiting for transfers between devices: 0.02 us -> 35.7 us  [body(): lax.psum_scatter(grad_out_weight, 'tensor', scatter_dimension=0, tiled=True)]
    psum x1, waiting for transfers between devices: 161 us -> 180 us  [body(): lax.psum(lax.psum_scatter(grad_out_weight, 'tensor', scatter_dimension=0,...]
    unnamed x83 -> x80, local copies, waits for them, and re-layouts: 28.7 us -> 27.8 us
  transfers between devices with their start and end apart: 10 -> 11, of which waited for: 8 -> 10; matrix products, arithmetic and copies ran while one was open for 20% -> 10% of each run, Pallas kernels for 0% -> 0%
where the time goes in v1:
time: 938 us; the launch traced here: 930 us
  waiting for transfers between devices  614 us (65%)
  matrix products  122 us (13%)
  blocking collectives  89.3 us (10%)
  local copies, waits for them, and re-layouts  62.2 us (7%)
  other arithmetic  25.6 us (3%)
  between operations  15.6 us (2%)
    psum x1, waiting for transfers between devices, body(): lax.psum(lax.psum_scatter(grad_out_weight, 'tensor', scatter_dimension=0,...  180 us
    all_gather x1, waiting for transfers between devices, body(): grad_qkv = lax.all_gather(array_here, axis_name='dp').sum(axis=0)  124 us
    reduce_scatter x1, waiting for transfers between devices, body(): lax.psum_scatter(grad_down, 'tensor', scatter_dimension=0, tiled=True)  80.6 us
    reduce_scatter x1, waiting for transfers between devices, body(): lax.psum_scatter(grad_up, 'tensor', scatter_dimension=0, tiled=True)  80.6 us
    psum x1, blocking collectives, body(): lax.psum((grad_out_bias, grad_gain_mid, grad_shift_mid, grad_down_bias, g...  45.4 us
    reduce_scatter x1, waiting for transfers between devices, body(): lax.psum_scatter(grad_out_weight, 'tensor', scatter_dimension=0, tiled=True)  35.7 us
    all_gather x1, waiting for transfers between devices, body(): w_up = lax.all_gather(up_weight, 'tensor', axis=0, tiled=True)  34.8 us
    reduce_scatter x1, waiting for transfers between devices, body(): lax.psum_scatter(grad_qkv, 'tensor', scatter_dimension=1, tiled=True)  31.8 us
  transfers between devices with their start and end apart: 11, of which 10 were waited for; matrix products, arithmetic and copies ran while one was open for 10% of the time, Pallas kernels for 0%

profile of v1, /device:TPU:0, one launch (start us, length us, event | category | flops | bytes accessed | tf_op | source)
XLA Modules:
  0.0 929.5 jit_solution(15874388353317299020)
XLA Ops:
  10.3 6.0 all-gather.1
  18.9 5.5 all-gather.2
  26.2 16.9 %all-gather.9.cloned.1.call-done = bf16[3,768,768]{2,1,0:T(8,128)(2,1)} async-done(((bf16[3,192,768]{2,1,0:T(8,128)(2,1)}), bf16[3,768,768]{2,1,0:T(8,128)(2,1)}) %all-gather.9.cloned.1.call-update) | async-done | bytes 3538960 | tf_op jit(solution)/shard_map/all_gather | solution.py:63
  43.2 6.1 fusion.8
  53.1 2.7 fusion.64
  58.4 2.4 copy.86
  62.2 3.8 fusion.65
  66.4 34.8 %all-gather.13.cloned.1.call-done = bf16[3072,768]{1,0:T(8,128)(2,1)} async-done(((bf16[768,768]{1,0:T(8,128)(2,1)}), bf16[3072,768]{1,0:T(8,128)(2,1)}) %all-gather.13.cloned.1.call-update) | async-done | bytes 4718608 | tf_op jit(solution)/shard_map/all_gather | solution.py:66
  101.2 13.0 %multiply_convert_fusion = (bf16[1024,3072]{1,0:T(8,128)(2,1)}, f32[1024,3072]{1,0:T(8,128)}) fusion(f32[3072]{0:T(1024)S(1)} %bitcast.119, bf16[3072,768]{1,0:T(8,128)(2,1)} %all-gather.13.cloned.1.call-done, f32[1024,768]{0,1:T(8,128)S(1)} %get-tuple-element.91, f32[768]{0:T(1024)S(1)} %convert_element_type.102, f32[768]{0:T(1024)S(1)} %convert_element_type.101, ...), kind=kOutput, calls=%fused_computation.9 | convolution fusion | flops 4854644736 | bytes 26765312 | tf_op jit(solution)/shard_map/rd,fd->rf/dot_general | solution.py:103
  114.2 25.9 %all-gather.15.cloned.1.call-done = bf16[3072,768]{1,0:T(8,128)(2,1)} async-done(((bf16[768,768]{1,0:T(8,128)(2,1)}), bf16[3072,768]{1,0:T(8,128)(2,1)}) %all-gather.15.cloned.1.call-update) | async-done | bytes 4718608 | tf_op jit(solution)/shard_map/all_gather | solution.py:68
  140.1 9.4 %fusion.66 = (f32[1024]{0:T(1024)S(1)}, f32[1024,768]{0,1:T(8,128)S(1)}) fusion(f32[768]{0:T(1024)S(1)} %convert_element_type.106, bf16[1024,3072]{1,0:T(8,128)(2,1)} %get-tuple-element.92, bf16[3072,768]{1,0:T(8,128)(2,1)} %all-gather.15.cloned.1.call-done, f32[768]{0:T(1024)S(1)} %convert_element_type.102, f32[768]{0:T(1024)S(1)} %convert_element_type.101, ...), kind=kOutput, calls=%fused_computation.113 | convolution fusion | flops 4837342208 | bytes 17323008 | tf_op jit(solution)/shard_map/dot_general | solution.py:106
  152.4 12.6 %convert_reduce_fusion = (f32[3072]{0:T(1024)S(1)}, bf16[1024,3072]{1,0:T(8,128)(2,1)}) fusion(f32[1024,3072]{1,0:T(8,128)} %get-tuple-element.93, f32[3072]{0:T(1024)S(1)} %bitcast.120, bf16[3072,768]{1,0:T(8,128)(2,1)S(1)} %copy-done.24, f32[1024]{0:T(1024)S(1)} %get-tuple-element.101, f32[1024,768]{0,1:T(8,128)S(1)} %get-tuple-element.95, ...), kind=kOutput, calls=%fused_computation.8 | convolution fusion | flops 4880593920 | bytes 28359680 | tf_op jit(solution)/shard_map/rd,fd->rf/dot_general | solution.py:120
  165.0 10.8 %multiply_reduce_fusion.2 = (f32[768]{0:T(1024)S(1)}, f32[1024]{0:T(1024)S(1)}, f32[1024]{0:T(1024)S(1)}, f32[768]{0:T(1024)S(1)}, f32[1024,768]{0,1:T(8,128)S(1)}) fusion(f32[1024,768]{0,1:T(8,128)S(1)} %copy-done.6, f32[1024]{0:T(1024)S(1)} %add_rsqrt_fusion.1, f32[1024]{0:T(1024)S(1)} %broadcast_multiply_fusion.5, f32[768]{0:T(1024)S(1)} %convert_element_type.101, ...), kind=kOutput, calls=%fused_computation.23 | convolution fusion | flops 4846776320 | bytes 22069248 | tf_op jit(solution)/shard_map/dot_general | solution.py:128
  178.6 2.6 convolution_convert_fusion.1
  181.2 2.7 copy.90
  186.0 7.5 multiply_reduce_fusion
  193.6 5.0 multiply_convert_fusion.1
  199.9 3.4 fusion.26
  203.3 3.4 fusion.30
  206.8 2.4 copy.95
  209.2 3.7 stack_reshape.12
  212.9 2.6 copy.102
  215.5 3.8 copy.98
  219.3 3.7 stack_reshape.13
  222.9 2.8 copy.103
  225.7 3.8 copy.101
  229.5 3.7 stack_reshape.14
  233.2 2.6 copy.104
  235.7 9.7 %fusion.20 = f32[3,768,768]{2,1,0:T(8,128)} fusion(bf16[1024,768]{1,0:T(8,128)(2,1)} %param.17, bf16[1,1024,768]{2,1,0:T(8,128)(2,1)} %copy.104, bf16[1,1024,768]{2,1,0:T(8,128)(2,1)} %copy.103, bf16[1,1024,768]{2,1,0:T(8,128)(2,1)} %copy.102), kind=kOutput, calls=%fused_computation.58 | convolution fusion | flops 3628597248 | bytes 13369344 | tf_op jit(solution)/shard_map/crl,rd->cld/dot_general | solution.py:160
  245.5 5.2 fusion.17
  250.8 10.9 %fusion.47 = f32[3072,768]{1,0:T(8,128)} fusion(bf16[1024,3072]{1,0:T(8,128)(2,1)} %get-tuple-element.92, bf16[1024,768]{0,1:T(8,128)(2,1)} %copy.88, f32[1024,768]{0,1:T(8,128)S(1)} %get-tuple-element.95, f32[1024]{0:T(1024)S(1)} %get-tuple-element.101, f32[1024]{0:T(1024)S(1)} %get-tuple-element.102, f32[1024]{0:T(1024)S(1)} %get-tuple-element.86, ...), kind=kOutput, calls=%fused_computation.81 | convolution fusion | flops 4839702528 | bytes 20470784 | tf_op jit(solution)/shard_map/rf,rd->fd/dot_general | solution.py:116
  261.8 11.2 %fusion.56 = f32[3072,768]{1,0:T(8,128)} fusion(bf16[1024,3072]{1,0:T(8,128)(2,1)} %get-tuple-element.100, f32[1024,768]{0,1:T(8,128)} %copy-done.5, f32[768]{0:T(1024)S(1)} %convert_element_type.102, f32[768]{0:T(1024)S(1)} %convert_element_type.101, f32[1024]{0:T(1024)S(1)} %add_rsqrt_fusion.1, f32[1024]{0:T(1024)S(1)} %broadcast_multiply_fusion.5), kind=kOutput, calls=%fused_computation.105 | convolution fusion | flops 4835770368 | bytes 18888704 | tf_op jit(solution)/shard_map/rf,rd->fd/dot_general | solution.py:122
  273.1 2.7 convert_reduce_fusion.1
  276.8 31.8 %reduce-scatter.8.cloned.1.call-done = f32[3,192,768]{2,1,0:T(8,128)} async-done(((f32[3,768,768]{2,1,0:T(8,128)}), f32[3,192,768]{2,1,0:T(8,128)}) %reduce-scatter.8.cloned.1.call-update) | async-done | bytes 1769488 | tf_op jit(solution)/shard_map/reduce_scatter | solution.py:166
  308.7 35.7 %reduce-scatter.10.cloned.1.call-done = f32[192,768]{1,0:T(8,128)} async-done(((f32[768,768]{1,0:T(8,128)}), f32[192,768]{1,0:T(8,128)}) %reduce-scatter.10.cloned.1.call-update) | async-done | bytes 589840 | tf_op jit(solution)/shard_map/reduce_scatter | solution.py:136
  344.5 80.6 %reduce-scatter.14.cloned.1.call-done = f32[768,768]{1,0:T(8,128)} async-done(((f32[3072,768]{1,0:T(8,128)}), f32[768,768]{1,0:T(8,128)}) %reduce-scatter.14.cloned.1.call-update) | async-done | bytes 2359312 | tf_op jit(solution)/shard_map/reduce_scatter | solution.py:118
  425.0 80.6 %reduce-scatter.12.cloned.1.call-done = f32[768,768]{1,0:T(8,128)} async-done(((f32[3072,768]{1,0:T(8,128)}), f32[768,768]{1,0:T(8,128)}) %reduce-scatter.12.cloned.1.call-update) | async-done | bytes 2359312 | tf_op jit(solution)/shard_map/reduce_scatter | solution.py:124
  506.9 9.4 %fusion.9 = bf16[1024,768]{0,1:T(8,128)(2,1)} fusion(f32[1024,768]{0,1:T(8,128)} %copy-done.8, bf16[3,768,768]{2,1,0:T(8,128)(2,1)} %all-gather.9.cloned.1.call-done, bf16[1,1024,768]{2,1,0:T(8,128)(2,1)} %copy.104, bf16[1,1024,768]{2,1,0:T(8,128)(2,1)} %copy.103, bf16[1,1024,768]{2,1,0:T(8,128)(2,1)} %copy.102), kind=kOutput, calls=%fused_computation.21 | convolution fusion | flops 3630170112 | bytes 12976128 | tf_op jit(solution)/shard_map/crl,cld->rd/dot_general | solution.py:164
  516.3 2.6 copy.108
  518.8 4.2 multiply_reduce_fusion.1
  523.1 2.6 copy.107
  525.7 10.1 %all-reduce = f32[3072]{0:T(1024)S(1)} all-reduce(f32[3072]{0:T(1024)S(1)} %get-tuple-element.99), channel_id=7, replica_groups=mesh['dp'=8,'tensor'=4] {'tensor'}, use_global_device_ids=true, to_apply=%region_27.28.clone | all-reduce | flops 3072 | bytes 24576
  535.9 45.4 %all-reduce.1 = (f32[768]{0:T(1024)}, f32[768]{0:T(1024)}, f32[768]{0:T(1024)}, f32[768]{0:T(1024)}, f32[768]{0:T(1024)}, /*index=5*/f32[768]{0:T(1024)}) all-reduce(f32[768]{0:T(1024)S(1)} %get-tuple-element.76, f32[768]{0:T(1024)S(1)} %get-tuple-element.56, ...), channel_id=1, replica_groups=mesh['dp'=8,'tensor'=4] {'dp','tensor'}, use_global_device_ids=true, to_apply=%region_19.20 | all-reduce | flops 4608 | bytes 36864 | tf_op jit(solution)/shard_map/psum | solution.py:172
  582.3 22.3 %all-reduce.2 = (f32[2,192]{1,0:T(2,128)}, f32[768]{0:T(1024)}) all-reduce(f32[2,192]{1,0:T(2,128)S(1)} %copy.119, f32[768]{0:T(1024)S(1)} %dynamic-slice.1), channel_id=1, replica_groups=mesh['dp'=8,'tensor'=4] {'dp'}, use_global_device_ids=true, to_apply=%region_15.16 | all-reduce | flops 1152 | bytes 9216 | tf_op jit(solution)/shard_map/psum | solution.py:168
  604.5 123.9 %all-gather.17.cloned.1.call-done = f32[24,192,768]{2,1,0:T(8,128)} async-done(((f32[3,192,768]{2,1,0:T(8,128)}), f32[24,192,768]{2,1,0:T(8,128)}) %all-gather.17.cloned.1.call-update) | async-done | bytes 14155792 | tf_op jit(solution)/shard_map/all_gather | solution.py:167
  728.5 7.3 reduce_sum.181
  735.8 180.0 %all-reduce.6.cloned.1.call-done = (f32[192,768]{1,0:T(8,128)}, f32[768,768]{1,0:T(8,128)}, f32[768,768]{1,0:T(8,128)}) async-done(((f32[192,768]{1,0:T(8,128)}, f32[768,768]{1,0:T(8,128)}, f32[768,768]{1,0:T(8,128)}), (f32[192,768]{1,0:T(8,128)}, f32[768,768]{1,0:T(8,128)}, f32[768,768]{1,0:T(8,128)})) %all-reduce.6.cloned.1.call-update) | async-done | bytes 5308432 | tf_op jit(solution)/shard_map/psum | solution.py:135
  917.9 3.2 copy.159
  (133 shorter events, 30.9 us)
Async XLA Ops:
  7.2 3.0 copy-start.26
  7.2 3.0 copy-start.27
  7.2 3.1 copy-start.23
  7.2 10.0 %copy-start.11 = (bf16[1024,768]{1,0:T(8,128)(2,1)S(1)}, bf16[1024,768]{1,0:T(8,128)(2,1)}, u32[]{:S(2)}) copy-start(bf16[1024,768]{1,0:T(8,128)(2,1)} %param.17) | copy-start | bytes 4718596
  7.2 35.9 %all-gather.9.cloned.1.call-start = ((), (), s32[]{:S(2)}) async-start(), calls=%async_computation.5 | async-start | bytes 4423680 | tf_op jit(solution)/shard_map/all_gather | solution.py:63
  8.0 10.9 %copy-start.16 = (bf16[768]{0:T(1024)(128)(2,1)S(1)}, bf16[768]{0:T(1024)(128)(2,1)}, u32[]{:S(2)}) copy-start(bf16[768]{0:T(1024)(128)(2,1)} %param.21) | copy-start | bytes 4612
  8.0 10.9 %copy-start.17 = (bf16[768]{0:T(1024)(128)(2,1)S(1)}, bf16[768]{0:T(1024)(128)(2,1)}, u32[]{:S(2)}) copy-start(bf16[768]{0:T(1024)(128)(2,1)} %param.22) | copy-start | bytes 4612
  8.0 10.9 %copy-start.18 = (bf16[768]{0:T(1024)(128)(2,1)S(1)}, bf16[768]{0:T(1024)(128)(2,1)}, u32[]{:S(2)}) copy-start(bf16[768]{0:T(1024)(128)(2,1)} %param.23) | copy-start | bytes 4612
  8.0 10.9 %copy-start.22 = (bf16[768]{0:T(1024)(128)(2,1)S(1)}, bf16[768]{0:T(1024)(128)(2,1)}, u32[]{:S(2)}) copy-start(bf16[768]{0:T(1024)(128)(2,1)} %param.25) | copy-start | bytes 4612
  8.0 16.4 %copy-start.19 = (bf16[768]{0:T(1024)(128)(2,1)S(1)}, bf16[768]{0:T(1024)(128)(2,1)}, u32[]{:S(2)}) copy-start(bf16[768]{0:T(1024)(128)(2,1)} %param.27) | copy-start | bytes 4612
  8.0 16.4 %copy-start.10 = (bf16[1024,768]{1,0:T(8,128)(2,1)S(1)}, bf16[1024,768]{1,0:T(8,128)(2,1)}, u32[]{:S(2)}) copy-start(bf16[1024,768]{1,0:T(8,128)(2,1)} %param.30) | copy-start | bytes 4718596
  8.0 54.2 %all-gather.11.cloned.1.call-start = ((), (), s32[]{:S(2)}) async-start(), calls=%async_computation.6 | async-start | bytes 1474560 | tf_op jit(solution)/shard_map/all_gather | solution.py:65
  8.8 92.4 %all-gather.13.cloned.1.call-start = ((), (), s32[]{:S(2)}) async-start(), calls=%async_computation.7 | async-start | bytes 5898240 | tf_op jit(solution)/shard_map/all_gather | solution.py:66
  9.5 130.6 %all-gather.15.cloned.1.call-start = ((), (), s32[]{:S(2)}) async-start(), calls=%async_computation.8 | async-start | bytes 5898240 | tf_op jit(solution)/shard_map/all_gather | solution.py:68
  10.1 298.6 %reduce-scatter.8.cloned.1.call-start = ((), (), s32[]{:S(2)}) async-start(), calls=%async_computation.9 | async-start | bytes 8847360 | tf_op jit(solution)/shard_map/reduce_scatter | solution.py:166
  17.2 8.9 copy-start.20
  50.8 1.2 copy-start
  51.3 1.8 copy-start.2
  51.7 4.0 copy-start.12
  55.8 2.6 copy-start.7
  66.0 48.2 %copy-start.5 = (f32[1024,768]{0,1:T(8,128)}, f32[1024,768]{0,1:T(8,128)S(1)}, u32[]{:S(2)}) copy-start(f32[1024,768]{0,1:T(8,128)S(1)} %get-tuple-element.91) | copy-start | bytes 9437188
  149.5 1.4 copy-start.4
  149.9 2.5 copy-start.24
  152.4 12.6 %copy-start.6 = (f32[1024,768]{0,1:T(8,128)S(1)}, f32[1024,768]{0,1:T(8,128)}, u32[]{:S(2)}) copy-start(f32[1024,768]{0,1:T(8,128)} %copy-done.5) | copy-start | bytes 9437188
  175.9 2.8 copy-start.25
  177.0 1.6 copy-start.8
  184.0 2.0 copy-start.13
  186.0 7.6 copy-start.14
  186.0 7.6 slice-start
  186.0 7.5 slice-start.1
  193.5 5.0 copy-start.3
  198.5 1.4 copy-start.1
  199.9 3.4 copy-start.15
  245.5 99.0 %reduce-scatter.10.cloned.1.call-start = ((), (), s32[]{:S(2)}) async-start(), calls=%async_computation.10 | async-start | bytes 2949120 | tf_op jit(solution)/shard_map/reduce_scatter | solution.py:136
  250.8 174.3 %reduce-scatter.14.cloned.1.call-start = ((), (), s32[]{:S(2)}) async-start(), calls=%async_computation.12 | async-start | bytes 11796480 | tf_op jit(solution)/shard_map/reduce_scatter | solution.py:118
  261.8 243.8 %reduce-scatter.12.cloned.1.call-start = ((), (), s32[]{:S(2)}) async-start(), calls=%async_computation.11 | async-start | bytes 11796480 | tf_op jit(solution)/shard_map/reduce_scatter | solution.py:124
  273.1 308.2 %reduce-scatter.16.cloned.1.call-start = ((), (), s32[]{:S(2)}) async-start(), calls=%async_computation.14 | async-start | bytes 491520
  276.8 451.7 %all-gather.17.cloned.1.call-start = ((), (), s32[]{:S(2)}) async-start(), calls=%async_computation.13 | async-start | bytes 15925248 | tf_op jit(solution)/shard_map/all_gather | solution.py:167
  308.7 197.0 %copy-start.21 = (bf16[768]{0:T(1024)(128)(2,1)S(1)}, bf16[768]{0:T(1024)(128)(2,1)}, u32[]{:S(2)}) copy-start(bf16[768]{0:T(1024)(128)(2,1)} %param.29) | copy-start | bytes 4612
  308.7 197.0 %copy-start.28 = (u32[32]{0:T(128)S(1)}, u32[32]{0:T(128)}, u32[]{:S(2)}) copy-start(u32[32]{0:T(128)} %constant.52) | copy-start | bytes 388
  308.7 607.1 %all-reduce.6.cloned.1.call-start = ((), (), s32[]{:S(2)}) async-start(), calls=%async_computation.15 | async-start | bytes 10616832 | tf_op jit(solution)/shard_map/psum | solution.py:135
  915.8 5.3 copy-start.9
Sparse Core Ops, SparseCore 0:
  9.6 33.5 all-gather.8
  44.7 17.4 all-gather.10
  63.7 37.4 all-gather.12
  102.6 37.4 all-gather.14
  245.6 63.0 reduce-scatter.7
  311.6 32.8 reduce-scatter.9
  347.1 77.9 reduce-scatter.13
  427.6 77.9 reduce-scatter.11
  508.7 20.8 reduce-scatter.15
  531.6 196.8 all-gather.16
  732.5 183.2 all-reduce.5
